TPU v7x, 512 devices: a whole 4x8x8 slice. The times are simulated.
512 devices in a mesh: teach: 64 (over z, y), seq: 8 (over x, core).
Axes of the slice: x: 4, y: 8, z: 8, core: 2. Of those that a mesh axis runs over, the one named last changes fastest.
Arguments:
- teacher_in: bfloat16 [2048, 4, 5120], P('teach', None, 'seq'), may hold values from -6 to 6
- teacher_proj: bfloat16 [64, 5120, 512], P('teach', 'seq'), may hold values from -0.078125 to 0.078125
- family: int32 [2048, 4, 1], replicated, may hold values from 0 to 7; in each aligned block of 128 rows (0 to 127, 128 to 255, ..., all dimensions but the last counted through in order) at most 32 rows name the same one
- x_in: bfloat16 [2048, 4, 64, 64], P('seq', None, 'teach'), may hold values from -6 to 6
- b_in: bfloat16 [2048, 4, 64, 128], P('seq', None, 'teach'), may hold values from -1.796875 to 1.796875
- c_in: bfloat16 [2048, 4, 64, 128], P('seq', None, 'teach'), may hold values from -1.796875 to 1.796875
- step_size: float32 [2048, 4, 64], P('seq', None, 'teach'), may hold values from 0.02 to 0.1
- doc_start: int32 [2048, 4], P('seq'), may hold values from 0 to 1, as said below
- a_rate: float32 [64], P('teach'), may hold values from 0.001953125 to 1
- skip_gain: float32 [64], P('teach'), may hold values from 0.5 to 1.5
Outputs:
- grad_x: bfloat16 [2048, 4, 64, 64], P('seq', None, 'teach')
- grad_b: bfloat16 [2048, 4, 64, 128], P('seq', None, 'teach')
- grad_c: bfloat16 [2048, 4, 64, 128], P('seq', None, 'teach')
Inputs may be any that keep to these rules, and one draw needn't show every extreme that they name: In each source block of 128 rows no family appears more than 32 times, and in some source block some family appears exactly 32 times. `doc_start`: in each sequence exactly two ones: at position 0 and at one position from 512 up to 1536.
All inputs are finite; a program needn't handle non-finite values.
Results may differ from a plain program's by a relative error of at most 0.011.
Values may be sent and summed in bfloat16 or wider, within the bound.
No kernel may reach another device: no remote copies, remote signals or barrier semaphores. Data moves between devices by JAX's collectives and lax.ppermute only.
A program may use at most 64 MiB of HBM per device.

v0:
```python
import jax
import jax.numpy as jnp
from jax import lax
from jax.sharding import PartitionSpec as P

TD = 5120
P_SIZE = 64
FAM = 8
HEADS_DEV = 1
CAP = 32
EPS = 1e-06
HIGH = lax.Precision.HIGHEST
QUADRATIC = lax.Precision.HIGH


def prefix(value, axis, join, neutral, backward):
    count = lax.axis_size(axis)
    place = lax.axis_index(axis)
    ahead = count - 1 - place if backward else place
    gathered = jax.tree.map(
        lambda a, kind: lax.all_gather(a.astype(kind), axis), value, (jnp.bfloat16, jnp.bfloat16)
    )
    state = jax.tree.map(lambda a, e: jnp.zeros_like(a) + jnp.asarray(e, a.dtype), value, neutral)

    def one(hop, state):
        source = count - 1 - hop if backward else hop
        return join(
            state,
            jax.tree.map(
                lambda a, own: lax.dynamic_index_in_dim(a, source, 0, False).astype(own.dtype),
                gathered,
                value,
            ),
        )

    return lax.fori_loop(0, ahead, one, state)


def family_slots(fam_block):
    onehot = (fam_block[..., None] == jnp.arange(FAM, dtype=jnp.int32)[None, None, :]).astype(
        jnp.int32
    )
    before = jnp.cumsum(onehot, axis=1) - onehot
    return jnp.sum(before * onehot, axis=2)


def decay_matrix(log_sums, counts):
    places = jnp.arange(log_sums.shape[0])
    lower = places[:, None] >= places[None, :]
    same_doc = counts.T[:, :, None] == counts.T[:, None, :]
    keep_mask = (lower[None] & same_doc)[:, None]
    sums = log_sums.transpose(1, 2, 0)
    gaps = sums[:, :, :, None] - sums[:, :, None, :]
    return jnp.where(keep_mask, jnp.exp(jnp.where(keep_mask, gaps, 0.0)), 0.0)


def chain_combine(earlier, later):
    return (earlier[0] * later[0], later[0][:, :, None, None] * earlier[1] + later[1])


def per_device(
    teacher_in, teacher_proj, family, x_in, b_in, c_in, step_size, doc_start, a_rate, skip_gain
):
    teach_n = lax.axis_size("teach")
    seq_n = lax.axis_size("seq")
    owners = teach_n // FAM
    col_share = P_SIZE // (owners * seq_n)
    heads_all = HEADS_DEV * teach_n
    groups = teach_n // seq_n
    block_pos = teacher_in.shape[0]
    batch_n = teacher_in.shape[1]
    feat_width = teacher_in.shape[2]
    block_rows = block_pos * batch_n
    fam_all = family.reshape(family.shape[0] * family.shape[1])
    own_rows = teacher_in.reshape(block_rows, feat_width)
    own_fam = lax.dynamic_slice_in_dim(fam_all, lax.axis_index("teach") * block_rows, block_rows)
    slot_ids = family_slots(own_fam.reshape(1, block_rows))[0]
    dest_cols = own_fam * CAP + slot_ids
    select = (dest_cols[:, None] == jnp.arange(FAM * CAP, dtype=jnp.int32)[None, :]).astype(
        jnp.bfloat16
    )
    packed = jnp.dot(select.T, own_rows, preferred_element_type=jnp.float32).astype(jnp.bfloat16)
    outgoing = jnp.broadcast_to(
        packed.reshape(1, FAM, CAP, feat_width), (owners, FAM, CAP, feat_width)
    )
    outgoing = outgoing.reshape(teach_n, CAP, feat_width)
    weights = teacher_proj[0]
    received = lax.all_to_all(outgoing, "teach", split_axis=0, concat_axis=0, tiled=True)
    partial_value = jnp.einsum("tkf,fc->tkc", received, weights, preferred_element_type=jnp.float32)
    sq_sums = jnp.sum(jnp.square(received.astype(jnp.float32)), axis=2)
    partial_value, sq_sums = (partial_value, sq_sums)
    totals = lax.psum(sq_sums, "seq")
    row_scale = lax.rsqrt(totals / TD + EPS)
    scaled = (partial_value * row_scale[:, :, None]).reshape(
        teach_n, CAP, heads_all, seq_n, col_share
    )
    summed = lax.psum_scatter(scaled, "seq", scatter_dimension=3, tiled=True).astype(jnp.bfloat16)
    arrived = lax.all_to_all(
        lax.all_to_all(summed[None], "teach", split_axis=3, concat_axis=0, tiled=True),
        "seq",
        split_axis=1,
        concat_axis=4,
        tiled=True,
    )
    shard_rows = groups * block_rows
    shard_fam = lax.dynamic_slice_in_dim(
        fam_all, lax.axis_index("seq") * shard_rows, shard_rows
    ).reshape(groups, block_rows)
    shard_slots = family_slots(shard_fam)
    sources = jnp.arange(groups, dtype=jnp.int32)[:, None]
    row_index = ((shard_fam * groups + sources) * CAP + shard_slots).reshape(shard_rows)
    slot_table = arrived.reshape(owners, FAM, groups, CAP, HEADS_DEV, seq_n * col_share)
    slot_table = slot_table.transpose(1, 2, 3, 0, 4, 5).reshape(
        FAM * groups * CAP, owners, HEADS_DEV, seq_n * col_share
    )
    picked = jnp.take(slot_table, row_index, axis=0)
    target = picked.transpose(0, 2, 1, 3).reshape(groups * block_pos, batch_n, HEADS_DEV, P_SIZE)
    x_full = x_in.astype(jnp.float32)
    b_full = b_in.astype(jnp.float32)
    c_full = c_in.astype(jnp.float32)
    log_sums = jnp.cumsum(-step_size * a_rate[None, None, :], axis=0)
    counts = jnp.cumsum(doc_start, axis=0)
    same_end = (counts == counts[-1][None, :]).astype(jnp.float32)
    to_end = jnp.exp(log_sums[-1][None] - log_sums) * same_end[:, :, None]
    from_start = jnp.exp(log_sums) * (counts == 0).astype(jnp.float32)[:, :, None]
    through = jnp.exp(log_sums[-1]) * (counts[-1] == 0).astype(jnp.float32)[:, None]
    inputs = step_size[..., None] * x_full
    local_state = jnp.einsum("jbh,jbhp,jbhn->bhpn", to_end, inputs, b_full, precision=HIGH)
    start_ones = jnp.ones_like(through)
    _, state_in = prefix(
        (through, local_state),
        "seq",
        chain_combine,
        (start_ones, jnp.zeros_like(local_state)),
        False,
    )
    decay_mat = decay_matrix(log_sums, counts)
    scores = jnp.einsum("ibhn,jbhn->bhij", c_in, b_in, preferred_element_type=jnp.float32)
    mixing = decay_mat * scores
    output = jnp.einsum("bhij,jbhp->ibhp", mixing, inputs, precision=QUADRATIC)
    output = output + from_start[..., None] * jnp.einsum(
        "ibhn,bhpn->ibhp", c_full, state_in, precision=HIGH
    )
    output = output + skip_gain[None, None, :, None] * x_full
    residual = output - target.astype(jnp.float32)
    local_adjoint = jnp.einsum("ibh,ibhn,ibhp->bhnp", from_start, c_full, residual, precision=HIGH)
    _, adjoint_in = prefix(
        (through, local_adjoint),
        "seq",
        chain_combine,
        (start_ones, jnp.zeros_like(local_adjoint)),
        True,
    )
    grad_u = jnp.einsum("bhij,ibhp->jbhp", mixing, residual, precision=QUADRATIC)
    grad_u = grad_u + to_end[..., None] * jnp.einsum(
        "jbhn,bhnp->jbhp", b_full, adjoint_in, precision=HIGH
    )
    grad_x = step_size[..., None] * grad_u + skip_gain[None, None, :, None] * residual
    pair = decay_mat * jnp.einsum("ibhp,jbhp->bhij", residual, inputs, precision=QUADRATIC)
    grad_b = jnp.einsum("bhij,ibhn->jbhn", pair, c_full, precision=QUADRATIC)
    grad_b = grad_b + to_end[..., None] * jnp.einsum(
        "jbhp,bhnp->jbhn", inputs, adjoint_in, precision=HIGH
    )
    grad_c = jnp.einsum("bhij,jbhn->ibhn", pair, b_full, precision=QUADRATIC)
    grad_c = grad_c + from_start[..., None] * jnp.einsum(
        "ibhp,bhpn->ibhn", residual, state_in, precision=HIGH
    )
    return (grad_x.astype(jnp.bfloat16), grad_b.astype(jnp.bfloat16), grad_c.astype(jnp.bfloat16))


def solution(mesh):
    placed = (
        P("teach", None, "seq"),
        P("teach", "seq", None),
        P(),
        P("seq", None, "teach", None),
        P("seq", None, "teach", None),
        P("seq", None, "teach", None),
        P("seq", None, "teach"),
        P("seq", None),
        P("teach"),
        P("teach"),
    )
    return jax.shard_map(
        per_device,
        mesh=mesh,
        in_specs=placed,
        out_specs=(
            P("seq", None, "teach", None),
            P("seq", None, "teach", None),
            P("seq", None, "teach", None),
        ),
        check_vma=False,
    )
```

profile of v0, /device:TPU:1, one launch (start us, length us, event | category | flops | bytes accessed | tf_op | source)
XLA Modules:
  0.0 285.0 jit_solution(6432824276978671787)
XLA Ops:
  11.3 79.0 %all_to_all.38 = bf16[64,32,640]{2,1,0:T(8,128)(2,1)S(1)} all-to-all(bf16[64,32,640]{2,1,0:T(8,128)(2,1)S(1)} %bitcast.257), channel_id=1, replica_groups=mesh['teach'=64,'seq'=8] {'teach'}, dimensions={0} | all-to-all | bytes 5242880 | tf_op jit(solution)/shard_map/all_to_all | solution.py:88
  90.8 23.5 %psum.7 = f32[64,32]{1,0:T(8,128)S(1)} all-reduce(f32[64,32]{1,0:T(8,128)S(1)} %multiply_reduce_fusion), channel_id=1, replica_groups=mesh['teach'=64,'seq'=8] {'seq'}, use_global_device_ids=true, to_apply=%region_11.12 | all-reduce | flops 2048 | bytes 16384 | tf_op jit(solution)/shard_map/psum | solution.py:92
  114.3 3.7 %convolution_multiply_fusion = f32[64,32,512]{2,1,0:T(8,128)} fusion(bf16[64,32,640]{2,1,0:T(8,128)(2,1)S(1)} %all_to_all.38, f32[64,32]{1,0:T(8,128)S(1)} %add_rsqrt_fusion, bf16[1,640,512]{2,1,0:T(8,128)(2,1)S(1)} %copy-done), kind=kOutput, calls=%fused_computation.7 | convolution fusion | flops 1343225856 | bytes 7479296 | tf_op jit(solution)/shard_map/tkf,fc->tkc/dot_general | solution.py:89
  118.1 6.9 %copy.294 = f32[64,32,512]{0,2,1:T(8,128)} copy(f32[64,32,512]{2,1,0:T(8,128)} %convolution_multiply_fusion) | data formatting | bytes 8388608 | tf_op jit(solution)/shard_map/mul | solution.py:94
  125.0 8.3 %copy.295 = f32[64,32,64,8,1]{2,1,4,0,3:T(8,128)} copy(f32[64,32,64,8,1]{0,3,2,1,4:T(8,128)} %bitcast.256) | data formatting | bytes 8388608 | tf_op jit(solution)/shard_map/reshape | solution.py:94
  134.1 1.2 reduce-window.16
  139.1 11.3 %all_gather.18 = bf16[8,4,1]{1,2,0:T(2,128)(2,1)S(1)} all-gather(bf16[1,4,1]{1,2,0:T(2,128)(2,1)S(1)} %get-tuple-element.260), channel_id=1, replica_groups=mesh['teach'=64,'seq'=8] {'seq'}, dimensions={0}, use_global_device_ids=true | all-gather | bytes 72 | tf_op jit(solution)/shard_map/all_gather | solution.py:21
  150.5 2.5 select_reduce_fusion
  154.0 13.8 %all-gather = bf16[32,64,128]{2,1,0:T(8,128)(2,1)S(1)} all-gather(bf16[4,64,128]{2,1,0:T(8,128)(2,1)S(1)} %convolution_convert_fusion.2), channel_id=2, replica_groups=mesh['teach'=64,'seq'=8] {'seq'}, dimensions={0}, use_global_device_ids=true | all-gather | bytes 589824 | tf_op jit(solution)/shard_map/all_gather | solution.py:21
  168.2 22.4 %reduce-scatter.2.cloned.1.call-done = f32[64,32,64,1,1]{2,1,4,0,3:T(8,128)} async-done(((f32[64,32,64,8,1]{2,1,4,0,3:T(8,128)}), f32[64,32,64,1,1]{2,1,4,0,3:T(8,128)}) %reduce-scatter.2.cloned.1.call-update) | async-done | bytes 524304 | tf_op jit(solution)/shard_map/reduce_scatter | solution.py:97
  190.6 1.3 fusion.22
  194.1 13.0 %all-to-all-start.1 = ((bf16[64,2,1024]{2,1,0:T(2,128)(2,1)}), bf16[64,2,1024]{2,1,0:T(2,128)(2,1)S(1)}, u32[]{:S(2)}, u32[]{:S(2)}) async-start(bf16[64,2,1024]{2,1,0:T(2,128)(2,1)} %reshape.443), calls=%async_computation.2 | async-start | bytes 524288 | tf_op jit(solution)/shard_map/all_to_all | solution.py:99
  207.7 11.8 %all-to-all-done.1 = bf16[64,2,1024]{2,1,0:T(2,128)(2,1)S(1)} async-done(((bf16[64,2,1024]{2,1,0:T(2,128)(2,1)}), bf16[64,2,1024]{2,1,0:T(2,128)(2,1)S(1)}, u32[]{:S(2)}, u32[]{:S(2)}) %all-to-all-start.1) | async-done | bytes 262176 | tf_op jit(solution)/shard_map/all_to_all | solution.py:99
  222.1 6.8 %all-to-all-start.2 = ((bf16[8,2,8192]{2,1,0:T(2,128)(2,1)}), bf16[8,2,8192]{2,1,0:T(2,128)(2,1)S(1)}, u32[]{:S(2)}, u32[]{:S(2)}) async-start(bf16[8,2,8192]{2,1,0:T(2,128)(2,1)} %reshape.445), calls=%async_computation.3 | async-start | bytes 524288 | tf_op jit(solution)/shard_map/all_to_all | solution.py:98
  228.9 1.3 convolution_bitcast_fusion.7
  233.4 2.0 all-to-all-done.2
  235.8 1.6 copy.299
  237.4 3.6 %copy.325 = bf16[8,8,32,8,1,8]{5,3,2,1,0,4:T(8,128)(2,1)} copy(bf16[8,8,32,8,1,8]{2,5,1,0,3,4:T(8,128)(2,1)S(1)} %bitcast.259) | data formatting | bytes 524288 | tf_op jit(solution)/shard_map/reshape | solution.py:113
  241.0 5.5 %gather_fusion = bf16[1024,8,8]{2,1,0:T(8,128)(2,1)S(1)} fusion(bf16[2048,8,8]{2,1,0:T(8,128)(2,1)} %bitcast.258, s32[1024]{0:T(1024)S(1)} %broadcast_clamp_fusion), kind=kCustom, calls=%fused_computation | custom fusion | bytes 266240 | tf_op jit(solution)/shard_map/jit(_take)/gather | solution.py:116
  246.6 1.4 gather.7
  248.2 1.4 fusion.11
  249.6 1.8 convolution_multiply_fusion.1
  255.5 14.0 %all-gather.1 = bf16[32,128,64]{1,2,0:T(8,128)(2,1)S(1)} all-gather(bf16[4,128,64]{1,2,0:T(8,128)(2,1)S(1)} %fusion.16), channel_id=3, replica_groups=mesh['teach'=64,'seq'=8] {'seq'}, dimensions={0}, use_global_device_ids=true | all-gather | bytes 589824 | tf_op jit(solution)/shard_map/all_gather | solution.py:21
  269.5 5.5 %while.27 = (s32[]{:T(128)}, f32[4,1,128,64]{3,2,1,0:T(8,128)S(1)}, s32[]{:T(128)}, bf16[8,4,1]{1,2,0:T(2,128)(2,1)}, bf16[8,4,1,128,64]{3,4,1,0,2:T(8,128)(2,1)...) while((s32[]{:T(128)}, f32[4,1,128,64]{3,2,1,0:T(8,128)S(1)}, s32[]{:T(128)}, ...), condition=%wide.region_14.15_spmd, body=%wide.region_13.14_spmd.sunk | while | flops 98314 | bytes 590011 | solution.py:36
  (129 shorter events, 30.5 us)
Async XLA Ops:
  7.2 107.2 %copy-start = (bf16[1,640,512]{2,1,0:T(8,128)(2,1)S(1)}, bf16[1,640,512]{2,1,0:T(8,128)(2,1)}, u32[]{:S(2)}) copy-start(bf16[1,640,512]{2,1,0:T(8,128)(2,1)} %param.15) | copy-start | bytes 1966084
  7.2 183.5 %reduce-scatter.2.cloned.1.call-start = ((), (), s32[]{:S(2)}) async-start(), calls=%async_computation.4 | async-start | bytes 9437184 | tf_op jit(solution)/shard_map/reduce_scatter | solution.py:97
  9.1 144.7 %copy-start.8 = (s32[8192]{0:T(1024)}, s32[8192]{0:T(1024)S(1)}, u32[]{:S(2)}) copy-start(s32[8192]{0:T(1024)S(1)} %reshape.413) | copy-start | bytes 98308
  133.3 0.8 copy-start.11
  133.3 2.2 copy-start.14
  133.3 20.4 %copy-start.4 = (bf16[256,4,1,64]{0,3,2,1:T(8,128)(2,1)S(1)}, bf16[256,4,1,64]{0,3,2,1:T(8,128)(2,1)}, u32[]{:S(2)}) copy-start(bf16[256,4,1,64]{0,3,2,1:T(8,128)(2,1)} %param.17) | copy-start | bytes 393220
  133.3 20.5 %copy-start.5 = (bf16[256,4,1,128]{3,1,2,0:T(4,128)(2,1)S(1)}, bf16[256,4,1,128]{3,1,2,0:T(4,128)(2,1)}, u32[]{:S(2)}) copy-start(bf16[256,4,1,128]{3,1,2,0:T(4,128)(2,1)} %param.18) | copy-start | bytes 786436
  137.2 70.0 %copy-start.9 = (s32[1,4,2,128]{3,1,2,0:T(4,128)}, s32[1,4,2,128]{3,1,2,0:T(4,128)S(1)}, u32[]{:S(2)}) copy-start(s32[1,4,2,128]{3,1,2,0:T(4,128)S(1)} %copy.357) | copy-start | bytes 12292
  139.0 68.2 %copy-start.3 = (bf16[256,4,1,128]{3,1,2,0:T(4,128)(2,1)S(1)}, bf16[256,4,1,128]{3,1,2,0:T(4,128)(2,1)}, u32[]{:S(2)}) copy-start(bf16[256,4,1,128]{3,1,2,0:T(4,128)(2,1)} %param.19) | copy-start | bytes 786436
  168.2 51.3 %copy-start.13 = (bf16[8,4,1]{1,2,0:T(2,128)(2,1)}, bf16[8,4,1]{1,2,0:T(2,128)(2,1)S(1)}, u32[]{:S(2)}) copy-start(bf16[8,4,1]{1,2,0:T(2,128)(2,1)S(1)} %get-tuple-element.386) | copy-start | bytes 196
  194.1 25.5 %all-to-all-start.1 = ((bf16[64,2,1024]{2,1,0:T(2,128)(2,1)}), bf16[64,2,1024]{2,1,0:T(2,128)(2,1)S(1)}, u32[]{:S(2)}, u32[]{:S(2)}) async-start(bf16[64,2,1024]{2,1,0:T(2,128)(2,1)} %reshape.443), calls=%async_computation.2 | async-start | bytes 524288 | tf_op jit(solution)/shard_map/all_to_all | solution.py:99
  207.1 0.6 copy-start.7
  207.2 12.3 %copy-start.12 = (f32[4,256]{1,0:T(4,128)}, f32[4,256]{1,0:T(4,128)S(1)}, u32[]{:S(2)}) copy-start(f32[4,256]{1,0:T(4,128)S(1)} %bitcast_add_fusion) | copy-start | bytes 12292
  207.7 28.1 %copy-start.1 = (f32[4,256,256]{2,1,0:T(8,128)}, f32[4,256,256]{2,1,0:T(8,128)S(1)}, u32[]{:S(2)}) copy-start(f32[4,256,256]{2,1,0:T(8,128)S(1)} %convolution_multiply_fusion.2) | copy-start | bytes 3145732
  222.1 13.3 %all-to-all-start.2 = ((bf16[8,2,8192]{2,1,0:T(2,128)(2,1)}), bf16[8,2,8192]{2,1,0:T(2,128)(2,1)S(1)}, u32[]{:S(2)}, u32[]{:S(2)}) async-start(bf16[8,2,8192]{2,1,0:T(2,128)(2,1)} %reshape.445), calls=%async_computation.3 | async-start | bytes 524288 | tf_op jit(solution)/shard_map/all_to_all | solution.py:98
  241.0 8.6 %copy-start.10 = (s32[1,4,2,128]{3,1,2,0:T(4,128)S(1)}, s32[1,4,2,128]{3,1,2,0:T(4,128)}, u32[]{:S(2)}) copy-start(s32[1,4,2,128]{3,1,2,0:T(4,128)} %copy-done.9) | copy-start | bytes 12292
  248.0 3.5 %copy-start.6 = (bf16[256,4,1,128]{3,1,2,0:T(4,128)(2,1)S(1)}, bf16[256,4,1,128]{3,1,2,0:T(4,128)(2,1)}, u32[]{:S(2)}) copy-start(bf16[256,4,1,128]{3,1,2,0:T(4,128)(2,1)} %param.18) | copy-start | bytes 786436
  248.0 5.0 %copy-start.2 = (f32[4,256,256]{2,1,0:T(8,128)S(1)}, f32[4,256,256]{2,1,0:T(8,128)}, u32[]{:S(2)}) copy-start(f32[4,256,256]{2,1,0:T(8,128)} %copy-done.1) | copy-start | bytes 3145732
Sparse Core Ops, SparseCore 0:
  133.4 57.1 reduce-scatter.1
where the time goes:
time: 286 us; the launch traced here: 285 us
  blocking collectives  142 us (50%)
  local copies, waits for them, and re-layouts  41.9 us (15%)
  waiting for transfers between devices  36.2 us (13%)
  starting transfers between devices  19.9 us (7%)
  between operations  15.9 us (6%)
  matrix products  14.7 us (5%)
  other arithmetic  14.3 us (5%)
    all_to_all x1, blocking collectives, per_device(): lax.all_to_all(outgoing, 'teach', split_axis=0, concat_axis=0, tiled=True)  79 us
    all_gather x3, blocking collectives, prefix(): lax.all_gather(a.astype(kind), axis)  39.1 us
    psum x1, blocking collectives, per_device(): totals = lax.psum(sq_sums, 'seq')  23.5 us
    reduce_scatter x1, waiting for transfers between devices, per_device(): lax.psum_scatter(scaled, 'seq', scatter_dimension=3, tiled=True)  22.4 us
    all_to_all x1, starting transfers between devices, per_device(): lax.all_to_all(summed[None], 'teach', split_axis=3, concat_axis=0, tiled=...  13 us
    all_to_all x1, waiting for transfers between devices, per_device(): lax.all_to_all(summed[None], 'teach', split_axis=3, concat_axis=0, tiled=...  11.8 us
    reshape x1, local copies, waits for them, and re-layouts, per_device(): (partial_value * row_scale[:, :, None]).reshape(teach_n, CAP, heads_all,...  8.29 us
    gather x3, local copies, waits for them, and re-layouts, per_device(): picked = jnp.take(slot_table, row_index, axis=0)  7.08 us
  transfers between devices with their start and end apart: 3, of which 3 were waited for; matrix products, arithmetic and copies ran while one was open for 5% of the time, Pallas kernels for 0%

commit v1 on v0

--- a/solution.py
+++ b/solution.py
@@ -11,6 +11,29 @@
 EPS = 1e-06
 HIGH = lax.Precision.HIGHEST
 QUADRATIC = lax.Precision.HIGH
+
+
+def in_blocks(x, dim, size):
+    shape = x.shape
+    blocks = x.reshape(*shape[:dim], size, shape[dim] // size, *shape[dim + 1 :])
+    return jnp.moveaxis(blocks, dim, 0)
+
+
+def laid_out(blocks, dim):
+    blocks = jnp.moveaxis(blocks, 0, dim)
+    lengths = blocks.shape
+    return blocks.reshape(*lengths[:dim], lengths[dim] * lengths[dim + 1], *lengths[dim + 2 :])
+
+
+def exchange_in_pairs(array, axis, split_dim, concat_dim):
+    count, position = (lax.axis_size(axis), lax.axis_index(axis))
+    blocks = in_blocks(array, split_dim, count)
+    outs = [blocks[position]]
+    for lap in range(1, count):
+        sent = blocks[position ^ lap]
+        outs.append(lax.ppermute(sent, axis, [(i, i ^ lap) for i in range(count)]))
+    blocks = jnp.stack(outs)[position ^ jnp.arange(count)]
+    return laid_out(blocks, concat_dim)
 
 
 def prefix(value, axis, join, neutral, backward):
@@ -95,12 +118,8 @@
         teach_n, CAP, heads_all, seq_n, col_share
     )
     summed = lax.psum_scatter(scaled, "seq", scatter_dimension=3, tiled=True).astype(jnp.bfloat16)
-    arrived = lax.all_to_all(
-        lax.all_to_all(summed[None], "teach", split_axis=3, concat_axis=0, tiled=True),
-        "seq",
-        split_axis=1,
-        concat_axis=4,
-        tiled=True,
+    arrived = exchange_in_pairs(
+        lax.all_to_all(summed[None], "teach", split_axis=3, concat_axis=0, tiled=True), "seq", 1, 4
     )
     shard_rows = groups * block_rows
     shard_fam = lax.dynamic_slice_in_dim(

time: 286 us -> 300 us (1.049)
  starting transfers between devices: 19.9 us -> 37.8 us
  waiting for transfers between devices: 36.2 us -> 32.4 us
    ppermute x0 -> x7, starting transfers between devices: none -> 24.7 us  [exchange_in_pairs(): outs.append(lax.ppermute(sent, axis, [(i, i ^ lap) for i in range(count)]))]
    all_to_all x1 -> x0, starting transfers between devices: 6.84 us -> none  [per_device(): lax.all_to_all(lax.all_to_all(summed[None], 'teach', split_axis=3, concat...]
    all_to_all x1, waiting for transfers between devices: 11.8 us -> 8.17 us  [per_device(): lax.all_to_all(summed[None], 'teach', split_axis=3, concat_axis=0, tiled=...]
    ppermute x0 -> x7, waiting for transfers between devices: none -> 3.61 us  [exchange_in_pairs(): outs.append(lax.ppermute(sent, axis, [(i, i ^ lap) for i in range(count)]))]
  transfers between devices with their start and end apart: 3 -> 9, of which waited for: 3 -> 3; matrix products, arithmetic and copies ran while one was open for 5% -> 5% of each run, Pallas kernels for 0% -> 0%
where the time goes in v1:
time: 300 us; the launch traced here: 299 us
  blocking collectives  141 us (47%)
  local copies, waits for them, and re-layouts  40.3 us (13%)
  starting transfers between devices  37.8 us (13%)
  waiting for transfers between devices  32.4 us (11%)
  between operations  16.1 us (5%)
  other arithmetic  15.6 us (5%)
  matrix products  15.4 us (5%)
    all_to_all x1, blocking collectives, per_device(): lax.all_to_all(outgoing, 'teach', split_axis=0, concat_axis=0, tiled=True)  79 us
    all_gather x3, blocking collectives, prefix(): lax.all_gather(a.astype(kind), axis)  38.3 us
    ppermute x7, starting transfers between devices, exchange_in_pairs(): outs.append(lax.ppermute(sent, axis, [(i, i ^ lap) for i in range(count)]))  24.7 us
    psum x1, blocking collectives, per_device(): totals = lax.psum(sq_sums, 'seq')  23.5 us
    reduce_scatter x1, waiting for transfers between devices, per_device(): lax.psum_scatter(scaled, 'seq', scatter_dimension=3, tiled=True)  20.6 us
    all_to_all x1, starting transfers between devices, per_device(): lax.all_to_all(summed[None], 'teach', split_axis=3, concat_axis=0, tiled=...  13 us
    reshape x1, local copies, waits for them, and re-layouts, per_device(): (partial_value * row_scale[:, :, None]).reshape(teach_n, CAP, heads_all,...  8.29 us
    all_to_all x1, waiting for transfers between devices, per_device(): lax.all_to_all(summed[None], 'teach', split_axis=3, concat_axis=0, tiled=...  8.17 us
  transfers between devices with their start and end apart: 9, of which 3 were waited for; matrix products, arithmetic and copies ran while one was open for 5% of the time, Pallas kernels for 0%

profile of v1, /device:TPU:1, one launch (start us, length us, event | category | flops | bytes accessed | tf_op | source)
XLA Modules:
  0.0 298.9 jit_solution(7774869487611370689)
XLA Ops:
  11.3 79.0 %all_to_all.20 = bf16[64,32,640]{2,1,0:T(8,128)(2,1)S(1)} all-to-all(bf16[64,32,640]{2,1,0:T(8,128)(2,1)S(1)} %bitcast.286), channel_id=1, replica_groups=mesh['teach'=64,'seq'=8] {'teach'}, dimensions={0} | all-to-all | bytes 5242880 | tf_op jit(solution)/shard_map/all_to_all | solution.py:111
  90.8 23.5 %psum.7 = f32[64,32]{1,0:T(8,128)S(1)} all-reduce(f32[64,32]{1,0:T(8,128)S(1)} %multiply_reduce_fusion), channel_id=1, replica_groups=mesh['teach'=64,'seq'=8] {'seq'}, use_global_device_ids=true, to_apply=%region_11.12 | all-reduce | flops 2048 | bytes 16384 | tf_op jit(solution)/shard_map/psum | solution.py:115
  114.3 3.7 %convolution_multiply_fusion = f32[64,32,512]{2,1,0:T(8,128)} fusion(bf16[64,32,640]{2,1,0:T(8,128)(2,1)S(1)} %all_to_all.20, f32[64,32]{1,0:T(8,128)S(1)} %add_rsqrt_fusion, bf16[1,640,512]{2,1,0:T(8,128)(2,1)S(1)} %copy-done), kind=kOutput, calls=%fused_computation.8 | convolution fusion | flops 1343225856 | bytes 7479296 | tf_op jit(solution)/shard_map/tkf,fc->tkc/dot_general | solution.py:112
  118.1 6.9 %copy.361 = f32[64,32,512]{0,2,1:T(8,128)} copy(f32[64,32,512]{2,1,0:T(8,128)} %convolution_multiply_fusion) | data formatting | bytes 8388608 | tf_op jit(solution)/shard_map/mul | solution.py:117
  125.0 8.3 %copy.362 = f32[64,32,64,8,1]{2,1,4,0,3:T(8,128)} copy(f32[64,32,64,8,1]{0,3,2,1,4:T(8,128)} %bitcast.285) | data formatting | bytes 8388608 | tf_op jit(solution)/shard_map/reshape | solution.py:117
  138.4 11.2 %all_gather.18 = bf16[8,4,1]{1,2,0:T(2,128)(2,1)} all-gather(bf16[1,4,1]{1,2,0:T(2,128)(2,1)S(1)} %get-tuple-element.280), channel_id=1, replica_groups=mesh['teach'=64,'seq'=8] {'seq'}, dimensions={0}, use_global_device_ids=true | all-gather | bytes 72 | tf_op jit(solution)/shard_map/all_gather | solution.py:44
  149.8 2.5 select_reduce_fusion
  154.0 13.8 %all-gather = bf16[32,64,128]{2,1,0:T(8,128)(2,1)S(1)} all-gather(bf16[4,64,128]{2,1,0:T(8,128)(2,1)S(1)} %convolution_convert_fusion.2), channel_id=2, replica_groups=mesh['teach'=64,'seq'=8] {'seq'}, dimensions={0}, use_global_device_ids=true | all-gather | bytes 589824 | tf_op jit(solution)/shard_map/all_gather | solution.py:44
  170.1 20.6 %reduce-scatter.2.cloned.1.call-done = f32[64,32,64,1,1]{2,1,4,0,3:T(8,128)} async-done(((f32[64,32,64,8,1]{2,1,4,0,3:T(8,128)}), f32[64,32,64,1,1]{2,1,4,0,3:T(8,128)}) %reduce-scatter.2.cloned.1.call-update) | async-done | bytes 524304 | tf_op jit(solution)/shard_map/reduce_scatter | solution.py:120
  194.1 13.0 %all-to-all-start.1 = ((bf16[64,2,1024]{2,1,0:T(2,128)(2,1)}), bf16[64,2,1024]{2,1,0:T(2,128)(2,1)S(1)}, u32[]{:S(2)}, u32[]{:S(2)}) async-start(bf16[64,2,1024]{2,1,0:T(2,128)(2,1)} %reshape.492), calls=%async_computation.2 | async-start | bytes 524288 | tf_op jit(solution)/shard_map/all_to_all | solution.py:122
  211.4 8.2 %all-to-all-done.1 = bf16[64,2,1024]{2,1,0:T(2,128)(2,1)S(1)} async-done(((bf16[64,2,1024]{2,1,0:T(2,128)(2,1)}), bf16[64,2,1024]{2,1,0:T(2,128)(2,1)S(1)}, u32[]{:S(2)}, u32[]{:S(2)}) %all-to-all-start.1) | async-done | bytes 262176 | tf_op jit(solution)/shard_map/all_to_all | solution.py:122
  221.1 5.4 %collective-permute-start = (bf16[64,8,32,1,1,1]{0,2,1,5,4,3:T(8,128)(2,1)S(1)}, bf16[64,8,32,1,1,1]{0,2,1,5,4,3:T(8,128)(2,1)S(1)}, u32[]{:S(2)}, u32[]{:S(2)}) collective-permute-start(bf16[64,8,32,1,1,1]{0,2,1,5,4,3:T(8,128)(2,1)S(1)} %get-tuple-element.278), channel_id=1, source_target_pairs={{0,1},{1,0},{2,3},{3,2},{4,5},{5,4},{6,7},{7,6},{8,9},{9,8},{10,11... | collective-permute-start | bytes 98312 | tf_op jit(solution)/shard_map/ppermute | solution.py:34
  226.5 2.0 collective-permute-start.1
  228.6 3.4 %collective-permute-start.2 = (bf16[64,8,32,1,1,1]{0,2,1,5,4,3:T(8,128)(2,1)S(1)}, bf16[64,8,32,1,1,1]{0,2,1,5,4,3:T(8,128)(2,1)S(1)}, u32[]{:S(2)}, u32[]{:S(2)}) collective-permute-start(bf16[64,8,32,1,1,1]{0,2,1,5,4,3:T(8,128)(2,1)S(1)} %get-tuple-element.276), channel_id=1, source_target_pairs={{0,3},{1,2},{2,1},{3,0},{4,7},{5,6},{6,5},{7,4},{8,11},{9,10},{10,... | collective-permute-start | bytes 98312 | tf_op jit(solution)/shard_map/ppermute | solution.py:34
  232.0 3.4 %collective-permute-start.3 = (bf16[64,8,32,1,1,1]{0,2,1,5,4,3:T(8,128)(2,1)S(1)}, bf16[64,8,32,1,1,1]{0,2,1,5,4,3:T(8,128)(2,1)S(1)}, u32[]{:S(2)}, u32[]{:S(2)}) collective-permute-start(bf16[64,8,32,1,1,1]{0,2,1,5,4,3:T(8,128)(2,1)S(1)} %get-tuple-element.275), channel_id=1, source_target_pairs={{0,4},{1,5},{2,6},{3,7},{4,0},{5,1},{6,2},{7,3},{8,12},{9,13},{10,... | collective-permute-start | bytes 98312 | tf_op jit(solution)/shard_map/ppermute | solution.py:34
  235.5 3.7 %collective-permute-start.4 = (bf16[64,8,32,1,1,1]{0,2,1,5,4,3:T(8,128)(2,1)S(1)}, bf16[64,8,32,1,1,1]{0,2,1,5,4,3:T(8,128)(2,1)S(1)}, u32[]{:S(2)}, u32[]{:S(2)}) collective-permute-start(bf16[64,8,32,1,1,1]{0,2,1,5,4,3:T(8,128)(2,1)S(1)} %get-tuple-element.274), channel_id=1, source_target_pairs={{0,5},{1,4},{2,7},{3,6},{4,1},{5,0},{6,3},{7,2},{8,13},{9,12},{10,... | collective-permute-start | bytes 98312 | tf_op jit(solution)/shard_map/ppermute | solution.py:34
  239.2 3.3 %collective-permute-start.5 = (bf16[64,8,32,1,1,1]{0,2,1,5,4,3:T(8,128)(2,1)S(1)}, bf16[64,8,32,1,1,1]{0,2,1,5,4,3:T(8,128)(2,1)S(1)}, u32[]{:S(2)}, u32[]{:S(2)}) collective-permute-start(bf16[64,8,32,1,1,1]{0,2,1,5,4,3:T(8,128)(2,1)S(1)} %get-tuple-element.273), channel_id=1, source_target_pairs={{0,6},{1,7},{2,4},{3,5},{4,2},{5,3},{6,0},{7,1},{8,14},{9,15},{10,... | collective-permute-start | bytes 98312 | tf_op jit(solution)/shard_map/ppermute | solution.py:34
  242.6 3.4 %collective-permute-start.6 = (bf16[64,8,32,1,1,1]{0,2,1,5,4,3:T(8,128)(2,1)S(1)}, bf16[64,8,32,1,1,1]{0,2,1,5,4,3:T(8,128)(2,1)S(1)}, u32[]{:S(2)}, u32[]{:S(2)}) collective-permute-start(bf16[64,8,32,1,1,1]{0,2,1,5,4,3:T(8,128)(2,1)S(1)} %get-tuple-element.272), channel_id=1, source_target_pairs={{0,7},{1,6},{2,5},{3,4},{4,3},{5,2},{6,1},{7,0},{8,15},{9,14},{10,... | collective-permute-start | bytes 98312 | tf_op jit(solution)/shard_map/ppermute | solution.py:34
  246.1 3.6 %collective-permute-done.6 = bf16[64,8,32,1,1,1]{0,2,1,5,4,3:T(8,128)(2,1)S(1)} collective-permute-done((bf16[64,8,32,1,1,1]{0,2,1,5,4,3:T(8,128)(2,1)S(1)}, bf16[64,8,32,1,1,1]{0,2,1,5,4,3:T(8,128)(2,1)S(1)}, u32[]{:S(2)}, u32[]{:S(2)}) %collective-permute-start.6) | collective-permute-done | bytes 32800 | tf_op jit(solution)/shard_map/ppermute | solution.py:34
  251.9 3.6 %copy.392 = bf16[8,8,32,8,1,8]{5,3,2,1,0,4:T(8,128)(2,1)} copy(bf16[8,8,32,8,1,8]{2,5,1,0,3,4:T(8,128)(2,1)S(1)} %bitcast.289) | data formatting | bytes 524288 | tf_op jit(solution)/shard_map/reshape | solution.py:132
  255.6 5.5 %gather_fusion.1 = bf16[1024,8,8]{2,1,0:T(8,128)(2,1)S(1)} fusion(bf16[2048,8,8]{2,1,0:T(8,128)(2,1)} %bitcast.287, s32[1024]{0:T(1024)S(1)} %copy-done.9), kind=kCustom, calls=%fused_computation.1 | custom fusion | bytes 266240 | tf_op jit(solution)/shard_map/jit(_take)/gather | solution.py:135
  264.2 1.8 convolution_multiply_fusion.1
  270.0 13.2 %all-gather.1 = bf16[32,128,64]{1,2,0:T(8,128)(2,1)S(1)} all-gather(bf16[4,128,64]{1,2,0:T(8,128)(2,1)S(1)} %fusion.16), channel_id=3, replica_groups=mesh['teach'=64,'seq'=8] {'seq'}, dimensions={0}, use_global_device_ids=true | all-gather | bytes 589824 | tf_op jit(solution)/shard_map/all_gather | solution.py:44
  283.2 5.6 %while.27 = (s32[]{:T(128)}, f32[4,1,128,64]{3,2,1,0:T(8,128)S(1)}, s32[]{:T(128)}, bf16[8,4,1]{1,2,0:T(2,128)(2,1)}, bf16[8,4,1,128,64]{3,4,1,0,2:T(8,128)(2,1)...) while((s32[]{:T(128)}, f32[4,1,128,64]{3,2,1,0:T(8,128)S(1)}, s32[]{:T(128)}, ...), condition=%wide.region_14.15_spmd, body=%wide.region_13.14_spmd.sunk | while | flops 98314 | bytes 590011 | solution.py:59
  (152 shorter events, 39.9 us)
Async XLA Ops:
  7.2 107.2 %copy-start = (bf16[1,640,512]{2,1,0:T(8,128)(2,1)S(1)}, bf16[1,640,512]{2,1,0:T(8,128)(2,1)}, u32[]{:S(2)}) copy-start(bf16[1,640,512]{2,1,0:T(8,128)(2,1)} %param.15) | copy-start | bytes 1966084
  7.2 183.5 %reduce-scatter.2.cloned.1.call-start = ((), (), s32[]{:S(2)}) async-start(), calls=%async_computation.3 | async-start | bytes 9437184 | tf_op jit(solution)/shard_map/reduce_scatter | solution.py:120
  9.1 144.1 %copy-start.8 = (s32[8192]{0:T(1024)}, s32[8192]{0:T(1024)S(1)}, u32[]{:S(2)}) copy-start(s32[8192]{0:T(1024)S(1)} %reshape.444) | copy-start | bytes 98308
  133.3 2.2 copy-start.15
  133.3 20.4 %copy-start.4 = (bf16[256,4,1,64]{0,3,2,1:T(8,128)(2,1)S(1)}, bf16[256,4,1,64]{0,3,2,1:T(8,128)(2,1)}, u32[]{:S(2)}) copy-start(bf16[256,4,1,64]{0,3,2,1:T(8,128)(2,1)} %param.17) | copy-start | bytes 393220
  133.3 20.4 %copy-start.5 = (bf16[256,4,1,128]{3,1,2,0:T(4,128)(2,1)S(1)}, bf16[256,4,1,128]{3,1,2,0:T(4,128)(2,1)}, u32[]{:S(2)}) copy-start(bf16[256,4,1,128]{3,1,2,0:T(4,128)(2,1)} %param.18) | copy-start | bytes 786436
  133.3 34.6 %copy-start.3 = (bf16[256,4,1,128]{3,1,2,0:T(4,128)(2,1)S(1)}, bf16[256,4,1,128]{3,1,2,0:T(4,128)(2,1)}, u32[]{:S(2)}) copy-start(bf16[256,4,1,128]{3,1,2,0:T(4,128)(2,1)} %param.19) | copy-start | bytes 786436
  137.2 0.9 copy-start.10
  153.1 40.0 %copy-start.7 = (pred[256,256]{1,0:T(8,128)(4,1)}, pred[256,256]{1,0:T(8,128)(4,1)S(1)}, u32[]{:S(2)}) copy-start(pred[256,256]{1,0:T(8,128)(4,1)S(1)} %iota_compare_fusion.2) | copy-start | bytes 196612
  153.7 37.0 %copy-start.13 = (f32[4,256]{1,0:T(4,128)}, f32[4,256]{1,0:T(4,128)S(1)}, u32[]{:S(2)}) copy-start(f32[4,256]{1,0:T(4,128)S(1)} %bitcast_add_fusion) | copy-start | bytes 12292
  167.9 39.3 %copy-start.14 = (pred[1024]{0:T(1024)(128)(4,1)S(1)}, pred[1024]{0:T(1024)(128)(4,1)}, u32[]{:S(2)}) copy-start(pred[1024]{0:T(1024)(128)(4,1)} %compare_and_fusion.1) | copy-start | bytes 3076
  169.1 50.8 %copy-start.1 = (f32[4,256,256]{2,1,0:T(8,128)}, f32[4,256,256]{2,1,0:T(8,128)S(1)}, u32[]{:S(2)}) copy-start(f32[4,256,256]{2,1,0:T(8,128)S(1)} %convolution_multiply_fusion.2) | copy-start | bytes 3145732
  194.1 25.5 %all-to-all-start.1 = ((bf16[64,2,1024]{2,1,0:T(2,128)(2,1)}), bf16[64,2,1024]{2,1,0:T(2,128)(2,1)S(1)}, u32[]{:S(2)}, u32[]{:S(2)}) async-start(bf16[64,2,1024]{2,1,0:T(2,128)(2,1)} %reshape.492), calls=%async_computation.2 | async-start | bytes 524288 | tf_op jit(solution)/shard_map/all_to_all | solution.py:122
  221.1 18.1 %collective-permute-start = (bf16[64,8,32,1,1,1]{0,2,1,5,4,3:T(8,128)(2,1)S(1)}, bf16[64,8,32,1,1,1]{0,2,1,5,4,3:T(8,128)(2,1)S(1)}, u32[]{:S(2)}, u32[]{:S(2)}) collective-permute-start(bf16[64,8,32,1,1,1]{0,2,1,5,4,3:T(8,128)(2,1)S(1)} %get-tuple-element.278), channel_id=1, source_target_pairs={{0,1},{1,0},{2,3},{3,2},{4,5},{5,4},{6,7},{7,6},{8,9},{9,8},{10,11... | collective-permute-start | bytes 98312 | tf_op jit(solution)/shard_map/ppermute | solution.py:34
  226.5 16.0 %collective-permute-start.1 = (bf16[64,8,32,1,1,1]{0,2,1,5,4,3:T(8,128)(2,1)S(1)}, bf16[64,8,32,1,1,1]{0,2,1,5,4,3:T(8,128)(2,1)S(1)}, u32[]{:S(2)}, u32[]{:S(2)}) collective-permute-start(bf16[64,8,32,1,1,1]{0,2,1,5,4,3:T(8,128)(2,1)S(1)} %get-tuple-element.277), channel_id=1, source_target_pairs={{0,2},{1,3},{2,0},{3,1},{4,6},{5,7},{6,4},{7,5},{8,10},{9,11},{10,... | collective-permute-start | bytes 98312 | tf_op jit(solution)/shard_map/ppermute | solution.py:34
  228.6 17.4 %collective-permute-start.2 = (bf16[64,8,32,1,1,1]{0,2,1,5,4,3:T(8,128)(2,1)S(1)}, bf16[64,8,32,1,1,1]{0,2,1,5,4,3:T(8,128)(2,1)S(1)}, u32[]{:S(2)}, u32[]{:S(2)}) collective-permute-start(bf16[64,8,32,1,1,1]{0,2,1,5,4,3:T(8,128)(2,1)S(1)} %get-tuple-element.276), channel_id=1, source_target_pairs={{0,3},{1,2},{2,1},{3,0},{4,7},{5,6},{6,5},{7,4},{8,11},{9,10},{10,... | collective-permute-start | bytes 98312 | tf_op jit(solution)/shard_map/ppermute | solution.py:34
  232.0 14.0 %collective-permute-start.3 = (bf16[64,8,32,1,1,1]{0,2,1,5,4,3:T(8,128)(2,1)S(1)}, bf16[64,8,32,1,1,1]{0,2,1,5,4,3:T(8,128)(2,1)S(1)}, u32[]{:S(2)}, u32[]{:S(2)}) collective-permute-start(bf16[64,8,32,1,1,1]{0,2,1,5,4,3:T(8,128)(2,1)S(1)} %get-tuple-element.275), channel_id=1, source_target_pairs={{0,4},{1,5},{2,6},{3,7},{4,0},{5,1},{6,2},{7,3},{8,12},{9,13},{10,... | collective-permute-start | bytes 98312 | tf_op jit(solution)/shard_map/ppermute | solution.py:34
  235.5 10.6 %collective-permute-start.4 = (bf16[64,8,32,1,1,1]{0,2,1,5,4,3:T(8,128)(2,1)S(1)}, bf16[64,8,32,1,1,1]{0,2,1,5,4,3:T(8,128)(2,1)S(1)}, u32[]{:S(2)}, u32[]{:S(2)}) collective-permute-start(bf16[64,8,32,1,1,1]{0,2,1,5,4,3:T(8,128)(2,1)S(1)} %get-tuple-element.274), channel_id=1, source_target_pairs={{0,5},{1,4},{2,7},{3,6},{4,1},{5,0},{6,3},{7,2},{8,13},{9,12},{10,... | collective-permute-start | bytes 98312 | tf_op jit(solution)/shard_map/ppermute | solution.py:34
  239.2 6.8 %collective-permute-start.5 = (bf16[64,8,32,1,1,1]{0,2,1,5,4,3:T(8,128)(2,1)S(1)}, bf16[64,8,32,1,1,1]{0,2,1,5,4,3:T(8,128)(2,1)S(1)}, u32[]{:S(2)}, u32[]{:S(2)}) collective-permute-start(bf16[64,8,32,1,1,1]{0,2,1,5,4,3:T(8,128)(2,1)S(1)} %get-tuple-element.273), channel_id=1, source_target_pairs={{0,6},{1,7},{2,4},{3,5},{4,2},{5,3},{6,0},{7,1},{8,14},{9,15},{10,... | collective-permute-start | bytes 98312 | tf_op jit(solution)/shard_map/ppermute | solution.py:34
  242.6 7.1 %collective-permute-start.6 = (bf16[64,8,32,1,1,1]{0,2,1,5,4,3:T(8,128)(2,1)S(1)}, bf16[64,8,32,1,1,1]{0,2,1,5,4,3:T(8,128)(2,1)S(1)}, u32[]{:S(2)}, u32[]{:S(2)}) collective-permute-start(bf16[64,8,32,1,1,1]{0,2,1,5,4,3:T(8,128)(2,1)S(1)} %get-tuple-element.272), channel_id=1, source_target_pairs={{0,7},{1,6},{2,5},{3,4},{4,3},{5,2},{6,1},{7,0},{8,15},{9,14},{10,... | collective-permute-start | bytes 98312 | tf_op jit(solution)/shard_map/ppermute | solution.py:34
  249.7 5.9 %copy-start.9 = (s32[1024]{0:T(1024)S(1)}, s32[1024]{0:T(1024)}, u32[]{:S(2)}) copy-start(s32[1024]{0:T(1024)} %broadcast_clamp_fusion) | copy-start | bytes 12292
  255.6 8.6 %copy-start.11 = (s32[1,4,2,128]{3,1,2,0:T(4,128)S(1)}, s32[1,4,2,128]{3,1,2,0:T(4,128)}, u32[]{:S(2)}) copy-start(s32[1,4,2,128]{3,1,2,0:T(4,128)} %copy-done.10) | copy-start | bytes 12292
  262.5 3.5 %copy-start.6 = (bf16[256,4,1,128]{3,1,2,0:T(4,128)(2,1)S(1)}, bf16[256,4,1,128]{3,1,2,0:T(4,128)(2,1)}, u32[]{:S(2)}) copy-start(bf16[256,4,1,128]{3,1,2,0:T(4,128)(2,1)} %param.18) | copy-start | bytes 786436
  262.5 5.0 %copy-start.2 = (f32[4,256,256]{2,1,0:T(8,128)S(1)}, f32[4,256,256]{2,1,0:T(8,128)}, u32[]{:S(2)}) copy-start(f32[4,256,256]{2,1,0:T(8,128)} %copy-done.1) | copy-start | bytes 3145732
  (1 other events, 0.8 us)
Sparse Core Ops, SparseCore 0:
  133.5 57.1 reduce-scatter.1
